TPU v7x, 32 devices: a whole 2x2x4 slice. The times are simulated.
32 devices in a mesh: clips: 2 (over y), patch: 4 (over z), span: 2 (over x), chan: 2 (over core).
Axes of the slice: x: 2, y: 2, z: 4, core: 2. Of those that a mesh axis runs over, the one named last changes fastest.
Arguments:
- latent_tiles: bfloat16 [4, 256, 4, 384], P(('clips', 'span'), 'patch'), parts along dimension 0, may hold values from -12 to 12
- route: int32 [4, 256], P(('clips', 'span')), parts along dimension 0, may hold values from 0 to 255, as said below
- w_query: bfloat16 [384, 384], replicated, may hold values from -0.5 to 4.6
- w_keyval: bfloat16 [384, 768], replicated, may hold values from -0.5 to 4.6
- conv_weight: bfloat16 [3, 3, 3, 384, 384], P(None, None, None, None, 'chan'), may hold values from -0.0625 to 0.0625
Outputs:
- decoded: bfloat16 [8, 8, 64, 384], P(('clips', 'span'), 'patch', None, 'chan'), parts along dimension 0
There are 2 independent parts, one for each index of `clips`. A program takes and returns all parts, laid end to end along the dimension named above; an argument that names none is the same for every part. Nothing has to cross between parts.
Inputs may be any that keep to these rules, and one draw needn't show every extreme that they name: `route`: each span's row is a permutation of 0 .. 255. The 64 tiles of positions j * 64 to (j + 1) * 64 - 1 go to at most 32 per owner, and in every span some such group sends exactly 32 to one owner.
All inputs are finite; a program needn't handle non-finite values.
Results may differ from a plain program's by a relative error of at most 0.0065.
Values may be sent and summed in bfloat16 or wider, within the bound.
No kernel may reach another device: no remote copies, remote signals or barrier semaphores. Data moves between devices by JAX's collectives and lax.ppermute only.
A program may use at most 64 MiB of HBM per device.

v0:
```python
import math
import jax
import jax.numpy as jnp
from jax import lax
from jax.sharding import PartitionSpec as P

C = 384
W = 64
RD = 2
FD = 2
epsilon = 1e-06


def scaled_rms(values):
    wide = values.astype(jnp.float32)
    return wide / jnp.sqrt(jnp.mean(wide * wide, axis=-1, keepdims=True) + epsilon)


def attend(queries, key_rows, value_rows):
    scale = 1.0 / math.sqrt(queries.shape[-1])
    scores = (
        jnp.einsum("fqc,fkc->fqk", queries, key_rows, preferred_element_type=jnp.float32) * scale
    )
    largest = jnp.max(scores, axis=-1, keepdims=True)
    powers = jnp.exp(scores - largest)
    totals = jnp.sum(powers, axis=-1, keepdims=True)
    weights = powers.astype(jnp.bfloat16)
    summed = jnp.einsum("fqk,fkc->fqc", weights, value_rows, preferred_element_type=jnp.float32)
    return summed / totals


def spatial_conv(frames, kernel):
    return lax.conv_general_dilated(
        frames,
        kernel,
        (1, 1),
        ((0, 0), (1, 1)),
        dimension_numbers=("NHWC", "HWIO", "NHWC"),
        preferred_element_type=jnp.float32,
    )


def local(latent_tiles, route, w_query, w_keyval, conv_weight):
    patch_count = lax.axis_size("patch")
    patch_index = lax.axis_index("patch")
    chan_count = lax.axis_size("chan")
    chan_index = lax.axis_index("chan")
    span_count = lax.axis_size("span")
    table = route[0]
    block = latent_tiles.shape[1]
    share = block // chan_count
    own_share = lax.dynamic_slice_in_dim(latent_tiles, chan_index * share, share, 1)
    every_tile = lax.all_gather(own_share, ("patch", "chan"), axis=1, tiled=True)[0]
    tile_total = every_tile.shape[0]
    rows = patch_count * RD
    inverse = (
        jnp.zeros((tile_total,), jnp.int32).at[table].set(jnp.arange(tile_total, dtype=jnp.int32))
    )
    placed = jnp.take(every_tile, inverse, axis=0).reshape(patch_count, FD, RD, W, C)
    whole = placed.transpose(1, 0, 2, 3, 4).reshape(FD, rows, W, C)
    normed_all = scaled_rms(whole).astype(jnp.bfloat16)
    padded = jnp.pad(whole, ((0, 0), (1, 1), (0, 0), (0, 0)))
    features = lax.dynamic_slice_in_dim(padded, patch_index * RD, RD + 2, 1)
    normed = scaled_rms(features).astype(jnp.bfloat16)
    ext_cells = (RD + 2) * W
    queries = jnp.einsum(
        "fnc,cd->fnd", normed.reshape(FD, ext_cells, C), w_query, preferred_element_type=jnp.float32
    ).astype(jnp.bfloat16)
    keyvals = jnp.einsum(
        "fnc,cd->fnd",
        normed_all.reshape(FD, rows * W, C),
        w_keyval,
        preferred_element_type=jnp.float32,
    ).astype(jnp.bfloat16)
    attended = attend(queries, keyvals[..., :C], keyvals[..., C:])
    mixed = (features.astype(jnp.float32) + attended.reshape(FD, RD + 2, W, C)).astype(jnp.bfloat16)
    row_ids = patch_index * RD - 1 + jnp.arange(RD + 2)
    inside = ((row_ids >= 0) & (row_ids < rows))[None, :, None, None]
    activated = jnp.where(inside, jax.nn.silu(scaled_rms(mixed)), 0.0).astype(jnp.bfloat16)
    tap_sums = [spatial_conv(activated, conv_weight[a]) for a in range(3)]
    to_next = jnp.stack([tap_sums[0][0] + tap_sums[1][1], tap_sums[0][1]])
    pairs = [(i, i + 1) for i in range(span_count - 1)]
    from_prev = lax.ppermute(to_next, "span", pairs)
    own_sum = jnp.stack([tap_sums[2][0], tap_sums[1][0] + tap_sums[2][1]])
    out_width = conv_weight.shape[-1]
    own_rows = mixed[:, 1 : RD + 1]
    own_channels = lax.dynamic_slice_in_dim(own_rows, chan_index * out_width, out_width, 3)
    return (own_channels.astype(jnp.float32) + own_sum + from_prev).astype(jnp.bfloat16)


def solution(mesh):
    placed = (
        P(("clips", "span"), "patch", None, None),
        P(("clips", "span"), None),
        P(),
        P(),
        P(None, None, None, None, "chan"),
    )
    return jax.shard_map(
        local,
        mesh=mesh,
        in_specs=placed,
        out_specs=P(("clips", "span"), "patch", None, "chan"),
        check_vma=False,
    )
```

profile of v0, /device:TPU:0, one launch (start us, length us, event | category | flops | bytes accessed | tf_op | source)
XLA Modules:
  0.0 45.3 jit_solution(2556529948983996494)
XLA Ops:
  0.0 0.0 copy-start
  0.0 0.7 %compare_select_fusion.1 = s32[256,1]{0,1:T(1,128)S(1)} fusion(s32[1,256]{1,0:T(1,128)} %param.6), kind=kLoop, calls=%fused_computation.61 | loop fusion | flops 768 | bytes 2048 | tf_op jit(solution)/shard_map/select_n | solution.py:57
  0.8 1.4 %scatter_custom_fusion = s32[256]{0:T(256)S(1)} fusion(s32[256]{0:T(256)S(1)} %bitcast.81, s32[256]{0:T(256)S(1)} %iota.8, s32[]{:T(128)} %constant.22.clone.1), kind=kCustom, calls=%fused_computation.69 | custom fusion | bytes 1028 | tf_op jit(solution)/shard_map/scatter | solution.py:57
  2.2 0.1 broadcast_in_dim.37
  2.3 0.1 broadcast_in_dim.38
  2.4 0.1 broadcast_in_dim.39
  2.6 0.9 %constant_dynamic-slice_fusion = bf16[1,32,4,384]{3,2,0,1:T(4,128)(2,1)S(1)} fusion(bf16[1,64,4,384]{3,2,0,1:T(4,128)(2,1)} %bitcast.80, s32[]{:T(128)S(6)} %select_n.35), kind=kLoop, calls=%fused_computation.68 | loop fusion | bytes 196612 | tf_op jit(solution)/shard_map/dynamic_slice | solution.py:52
  3.5 17.2 %all_gather.3 = bf16[1,256,4,384]{3,2,0,1:T(4,128)(2,1)S(1)} all-gather(bf16[1,32,4,384]{3,2,0,1:T(4,128)(2,1)S(1)} %constant_dynamic-slice_fusion), channel_id=1, replica_groups=mesh['clips'=2,'patch'=4,'span'=2,'chan'=2] {'patch','chan'}, dimensions={1}, use_global_device_ids=true | all-gather | bytes 884736 | tf_op jit(solution)/shard_map/all_gather | solution.py:53
  20.7 1.5 %gather_fusion = bf16[256,4,384]{2,1,0:T(4,128)(2,1)S(1)} fusion(bf16[256,4,384]{2,1,0:T(4,128)(2,1)S(1)} %bitcast.71, s32[1024]{0:T(1024)S(1)} %pad_clamp_fusion), kind=kCustom, calls=%fused_computation | custom fusion | bytes 1573888 | tf_op jit(solution)/shard_map/jit(_take)/gather | solution.py:59
  22.2 0.2 gather.7
  22.4 0.5 %multiply_reduce_fusion = (f32[2,4,2,64]{3,2,1,0:T(2,128)S(1)}, bf16[4,2,2,64,384]{4,3,2,0,1:T(8,128)(2,1)S(1)}) fusion(bf16[4,2,2,64,384]{4,3,2,1,0:T(8,128)(2,1)S(1)} %gather.7, pred[4,2,2,64]{3,2,0,1:T(4,128)(4,1)S(1)} %copy.32), kind=kLoop, calls=%fused_computation.6 | loop fusion | flops 1571840 | bytes 1577984 | tf_op jit(solution)/shard_map/reduce_sum | solution.py:16
  22.9 0.1 sqrt.29
  23.0 0.2 bitcast_convert_fusion
  23.1 0.2 fusion.22
  23.3 0.2 fusion.23
  23.5 0.2 fusion
  23.7 0.0 copy-done
  23.7 0.0 copy-start.2
  23.7 2.1 %convolution_convert_fusion = bf16[2,512,768]{2,1,0:T(8,128)(2,1)} fusion(bf16[2,512,384]{2,1,0:T(8,128)(2,1)S(1)} %fusion, bf16[384,768]{1,0:T(8,128)(2,1)S(1)} %copy-done), kind=kOutput, calls=%fused_computation.3 | convolution fusion | flops 604766208 | bytes 2949120 | tf_op jit(solution)/shard_map/fnc,cd->fnd/dot_general | solution.py:69
  25.9 0.0 copy-done.2
  25.9 1.9 %fusion.46 = (f32[2,256]{1,0:T(2,128)S(1)}, f32[2,256,512]{2,1,0:T(8,128)S(1)}) fusion(bf16[2,512,768]{2,1,0:T(8,128)(2,1)} %convolution_convert_fusion, bf16[2,256,384]{2,1,0:T(8,128)(2,1)S(1)} %bitcast.79, bf16[384,384]{1,0:T(8,128)(2,1)S(1)} %copy-done.2), kind=kOutput, calls=%fused_computation.72 | convolution fusion | flops 353041920 | bytes 2525184 | tf_op jit(solution)/shard_map/fqc,fkc->fqk/dot_general | solution.py:22
  27.8 0.3 fusion.19
  28.1 1.7 %convolution_divide_fusion = f32[2,256,384]{2,1,0:T(8,128)S(1)} fusion(bf16[2,512,768]{2,1,0:T(8,128)(2,1)} %convolution_convert_fusion, f32[2,256,512]{2,1,0:T(8,128)S(1)} %get-tuple-element.14, f32[2,256]{1,0:T(2,128)S(1)} %get-tuple-element.13, f32[2,256]{1,0:T(2,128)S(1)} %fusion.19), kind=kOutput, calls=%fused_computation.17 | convolution fusion | flops 202047488 | bytes 2625536 | tf_op jit(solution)/shard_map/fqk,fkc->fqc/dot_general | solution.py:28
  29.8 0.0 copy-start.1
  29.8 0.2 fusion.21
  30.1 0.3 fusion.37
  30.4 0.0 copy-start.3
  30.4 0.4 copy.46
  30.8 0.3 pad.5.clone
  31.2 0.1 slice.59
  31.2 0.5 %fusion.28 = bf16[4,2,8,11,384]{4,1,3,2,0:T(2,128)(2,1)S(1)} fusion(bf16[4,2,7,2,384]{4,1,3,2,0:T(2,128)(2,1)S(1)} %slice.59, bf16[4,2,8,9,384]{4,1,3,2,0:T(2,128)(2,1)S(1)} %bitcast.73), kind=kLoop, calls=%fused_computation.41 | loop fusion | flops 1622016 | bytes 1069056 | tf_op jit(solution)/shard_map/conv_general_dilated | solution.py:33
  31.7 0.2 copy-done.1
  31.9 0.0 copy-done.3
  31.9 0.7 %fusion.16 = f32[2,16,9,192]{3,1,2,0:T(8,128)S(1)} fusion(bf16[3,3,3,384,192]{3,4,2,1,0:T(8,128)(2,1)S(1)} %copy-done.1, bf16[4,2,8,11,384]{4,1,3,2,0:T(2,128)(2,1)S(1)} %fusion.28, pred[16,9]{0,1:T(8,128)(4,1)S(1)} %copy-done.3), kind=kOutput, calls=%fused_computation.24 | convolution fusion | flops 382261248 | bytes 2091008 | tf_op jit(solution)/shard_map/conv_general_dilated | solution.py:33
  32.7 0.7 %fusion.13 = f32[2,16,9,192]{3,1,2,0:T(8,128)S(1)} fusion(bf16[3,3,3,384,192]{3,4,2,1,0:T(8,128)(2,1)S(1)} %copy-done.1, bf16[4,2,8,11,384]{4,1,3,2,0:T(2,128)(2,1)S(1)} %fusion.28, pred[16,9]{0,1:T(8,128)(4,1)S(1)} %copy-done.3), kind=kOutput, calls=%fused_computation.23 | convolution fusion | flops 382261248 | bytes 2091008 | tf_op jit(solution)/shard_map/conv_general_dilated | solution.py:33
  33.4 0.7 %fusion.10 = f32[2,16,9,192]{3,1,2,0:T(8,128)S(1)} fusion(bf16[3,3,3,384,192]{3,4,2,1,0:T(8,128)(2,1)S(1)} %copy-done.1, bf16[4,2,8,11,384]{4,1,3,2,0:T(2,128)(2,1)S(1)} %fusion.28, pred[16,9]{0,1:T(8,128)(4,1)S(1)} %copy-done.3), kind=kOutput, calls=%fused_computation.22 | convolution fusion | flops 382261248 | bytes 2091008 | tf_op jit(solution)/shard_map/conv_general_dilated | solution.py:33
  34.1 0.2 copy.41
  34.4 0.2 copy.37
  34.7 0.2 copy.39
  35.0 0.1 fusion.45
  35.1 3.4 %collective-permute-start = (f32[2,2,64,192]{3,2,1,0:T(8,128)S(1)}, f32[2,2,64,192]{3,2,1,0:T(8,128)S(1)}, u32[]{:S(2)}, u32[]{:S(2)}) collective-permute-start(f32[2,2,64,192]{3,2,1,0:T(8,128)S(1)} %pad_maximum_fusion), channel_id=1, source_target_pairs={{0,2},{1,3},{4,6},{5,7},{8,10},{9,11},{12,14},{13,15},{16,18},{17,... | collective-permute-start | bytes 589832 | tf_op jit(solution)/shard_map/ppermute | solution.py:83
  38.6 6.0 %collective-permute-done = f32[2,2,64,192]{3,2,1,0:T(8,128)S(1)} collective-permute-done((f32[2,2,64,192]{3,2,1,0:T(8,128)S(1)}, f32[2,2,64,192]{3,2,1,0:T(8,128)S(1)}, u32[]{:S(2)}, u32[]{:S(2)}) %collective-permute-start) | collective-permute-done | bytes 196640 | tf_op jit(solution)/shard_map/ppermute | solution.py:83
  44.5 0.8 %fusion.41 = bf16[2,2,64,192]{3,2,1,0:T(8,128)(2,1)} fusion(f32[2,2,64,192]{3,2,1,0:T(8,128)S(1)} %collective-permute-done, f32[1,2,64,192]{3,2,1,0:T(8,128)S(1)} %get-tuple-element.10, f32[1,2,64,192]{3,2,1,0:T(8,128)S(1)} %get-tuple-element.9, bf16[2,2,64,384]{3,2,1,0:T(8,128)(2,1)S(1)} %slice.58, s32[]{:T(128)S(6)} %select_n.38), kind=kLoop, calls=%fused_computation.53 | loop fusion | flops 245760 | bytes 589828 | tf_op jit(solution)/shard_map/convert_element_type | solution.py:88
  (17 shorter events, 0.2 us)
Async XLA Ops:
  0.0 23.7 %copy-start = (bf16[384,768]{1,0:T(8,128)(2,1)S(1)}, bf16[384,768]{1,0:T(8,128)(2,1)}, u32[]{:S(2)}) copy-start(bf16[384,768]{1,0:T(8,128)(2,1)} %param.8) | copy-start | bytes 1769476
  23.7 2.1 %copy-start.2 = (bf16[384,384]{1,0:T(8,128)(2,1)S(1)}, bf16[384,384]{1,0:T(8,128)(2,1)}, u32[]{:S(2)}) copy-start(bf16[384,384]{1,0:T(8,128)(2,1)} %param.7) | copy-start | bytes 884740
  29.8 2.1 %copy-start.1 = (bf16[3,3,3,384,192]{3,4,2,1,0:T(8,128)(2,1)S(1)}, bf16[3,3,3,384,192]{3,4,2,1,0:T(8,128)(2,1)}, u32[]{:S(2)}) copy-start(bf16[3,3,3,384,192]{3,4,2,1,0:T(8,128)(2,1)} %param.9) | copy-start | bytes 11943940
  30.4 1.5 %copy-start.3 = (pred[16,9]{0,1:T(8,128)(4,1)S(1)}, pred[16,9]{0,1:T(8,128)(4,1)}, u32[]{:S(2)}) copy-start(pred[16,9]{0,1:T(8,128)(4,1)} %constant.82) | copy-start | bytes 436
  35.1 9.5 %collective-permute-start = (f32[2,2,64,192]{3,2,1,0:T(8,128)S(1)}, f32[2,2,64,192]{3,2,1,0:T(8,128)S(1)}, u32[]{:S(2)}, u32[]{:S(2)}) collective-permute-start(f32[2,2,64,192]{3,2,1,0:T(8,128)S(1)} %pad_maximum_fusion), channel_id=1, source_target_pairs={{0,2},{1,3},{4,6},{5,7},{8,10},{9,11},{12,14},{13,15},{16,18},{17,... | collective-permute-start | bytes 589832 | tf_op jit(solution)/shard_map/ppermute | solution.py:83
where the time goes:
time: 45.6 us; the launch traced here: 45.3 us
  blocking collectives  17.2 us (38%)
  matrix products  7.88 us (17%)
  local copies, waits for them, and re-layouts  6.26 us (14%)
  waiting for transfers between devices  5.99 us (13%)
  other arithmetic  4.2 us (9%)
  starting transfers between devices  3.44 us (8%)
    all_gather x1, blocking collectives, local(): lax.all_gather(own_share, ('patch', 'chan'), axis=1, tiled=True)[0]  17.2 us
    ppermute x1, waiting for transfers between devices, local(): from_prev = lax.ppermute(to_next, 'span', pairs)  5.99 us
    ppermute x1, starting transfers between devices, local(): from_prev = lax.ppermute(to_next, 'span', pairs)  3.44 us
    conv_general_dilated x3, matrix products, spatial_conv(): lax.conv_general_dilated(frames, kernel, (1, 1), ((0, 0), (1, 1)), dimens...  2.15 us
    dot_general x1, matrix products, local(): jnp.einsum('fnc,cd->fnd', normed_all.reshape(FD, rows * W, C), w_keyval,...  2.13 us
    dot_general x1, matrix products, attend(): jnp.einsum('fqc,fkc->fqk', queries, key_rows, preferred_element_type=jnp....  1.93 us
    dot_general x1, matrix products, attend(): jnp.einsum('fqk,fkc->fqc', weights, value_rows, preferred_element_type=jn...  1.66 us
    gather x2, local copies, waits for them, and re-layouts, local(): jnp.take(every_tile, inverse, axis=0).reshape(patch_count, FD, RD, W, C)  1.65 us
  transfers between devices with their start and end apart: 1, of which 1 were waited for; matrix products, arithmetic and copies ran while one was open for 0% of the time, Pallas kernels for 0%

commit v1 on v0

--- a/solution.py
+++ b/solution.py
@@ -9,6 +9,18 @@
 RD = 2
 FD = 2
 epsilon = 1e-06
+
+
+def collect(x, axis, dim):
+    ways, here = (lax.axis_size(axis), lax.axis_index(axis))
+    grown, reach = (x, 1)
+    while reach < ways:
+        theirs = lax.ppermute(grown, axis, [(d, d ^ reach) for d in range(ways)])
+        mine_first = jnp.concatenate([grown, theirs], axis=dim)
+        theirs_first = jnp.concatenate([theirs, grown], axis=dim)
+        grown = jnp.where(here & reach == 0, mine_first, theirs_first)
+        reach = 2 * reach
+    return grown
 
 
 def scaled_rms(values):
@@ -50,7 +62,7 @@
     block = latent_tiles.shape[1]
     share = block // chan_count
     own_share = lax.dynamic_slice_in_dim(latent_tiles, chan_index * share, share, 1)
-    every_tile = lax.all_gather(own_share, ("patch", "chan"), axis=1, tiled=True)[0]
+    every_tile = collect(own_share, ("patch", "chan"), 1)[0]
     tile_total = every_tile.shape[0]
     rows = patch_count * RD
     inverse = (

time: 45.6 us -> 57.7 us (1.27)
  waiting for transfers between devices: 5.99 us -> 25.7 us
  blocking collectives: 17.2 us -> 0 us
  starting transfers between devices: 3.44 us -> 9.39 us
  other arithmetic: 4.2 us -> 6.32 us
  local copies, waits for them, and re-layouts: 6.26 us -> 7.25 us
    ppermute x0 -> x3, waiting for transfers between devices: none -> 21.1 us  [collect(): theirs = lax.ppermute(grown, axis, [(d, d ^ reach) for d in range(ways)])]
    all_gather x1 -> x0, blocking collectives: 17.2 us -> none  [local(): lax.all_gather(own_share, ('patch', 'chan'), axis=1, tiled=True)[0]]
    ppermute x0 -> x3, starting transfers between devices: none -> 5.99 us  [collect(): theirs = lax.ppermute(grown, axis, [(d, d ^ reach) for d in range(ways)])]
    select_n x0 -> x5, other arithmetic: none -> 2.18 us  [collect(): grown = jnp.where(here & reach == 0, mine_first, theirs_first)]
    ppermute x1, waiting for transfers between devices: 5.99 us -> 4.64 us  [local(): from_prev = lax.ppermute(to_next, 'span', pairs)]
    concatenate x0 -> x1, local copies, waits for them, and re-layouts: none -> 0.93 us  [collect(): mine_first = jnp.concatenate([grown, theirs], axis=dim)]
  transfers between devices with their start and end apart: 1 -> 4, of which waited for: 1 -> 3; matrix products, arithmetic and copies ran while one was open for 0% -> 7% of each run, Pallas kernels for 0% -> 0%
where the time goes in v1:
time: 57.7 us; the launch traced here: 56.9 us
  waiting for transfers between devices  25.7 us (45%)
  starting transfers between devices  9.39 us (16%)
  matrix products  7.88 us (14%)
  local copies, waits for them, and re-layouts  7.25 us (13%)
  other arithmetic  6.32 us (11%)
    ppermute x3, waiting for transfers between devices, collect(): theirs = lax.ppermute(grown, axis, [(d, d ^ reach) for d in range(ways)])  21.1 us
    ppermute x3, starting transfers between devices, collect(): theirs = lax.ppermute(grown, axis, [(d, d ^ reach) for d in range(ways)])  5.99 us
    ppermute x1, waiting for transfers between devices, local(): from_prev = lax.ppermute(to_next, 'span', pairs)  4.64 us
    ppermute x1, starting transfers between devices, local(): from_prev = lax.ppermute(to_next, 'span', pairs)  3.4 us
    select_n x5, other arithmetic, collect(): grown = jnp.where(here & reach == 0, mine_first, theirs_first)  2.18 us
    conv_general_dilated x3, matrix products, spatial_conv(): lax.conv_general_dilated(frames, kernel, (1, 1), ((0, 0), (1, 1)), dimens...  2.16 us
    dot_general x1, matrix products, local(): jnp.einsum('fnc,cd->fnd', normed_all.reshape(FD, rows * W, C), w_keyval,...  2.14 us
    dot_general x1, matrix products, attend(): jnp.einsum('fqc,fkc->fqk', queries, key_rows, preferred_element_type=jnp....  1.94 us
  transfers between devices with their start and end apart: 4, of which 3 were waited for; matrix products, arithmetic and copies ran while one was open for 7% of the time, Pallas kernels for 0%

profile of v1, /device:TPU:0, one launch (start us, length us, event | category | flops | bytes accessed | tf_op | source)
XLA Modules:
  0.0 56.9 jit_solution(7492495593731533136)
XLA Ops:
  0.0 1.0 %constant_dynamic-slice_fusion = bf16[1,32,4,384]{3,2,1,0:T(4,128)(2,1)S(1)} fusion(bf16[1,64,4,384]{3,2,1,0:T(4,128)(2,1)} %param.5, s32[]{:T(128)S(6)} %select_n.102), kind=kLoop, calls=%fused_computation.73 | loop fusion | bytes 196612 | tf_op jit(solution)/shard_map/dynamic_slice | solution.py:64
  1.0 0.5 collective-permute-start
  1.5 0.7 %compare_select_fusion.1 = s32[256,1]{0,1:T(1,128)S(1)} fusion(s32[1,256]{1,0:T(1,128)} %param.6), kind=kLoop, calls=%fused_computation.66 | loop fusion | flops 768 | bytes 2048 | tf_op jit(solution)/shard_map/select_n | solution.py:69
  2.2 1.4 %scatter_custom_fusion = s32[256]{0:T(256)S(1)} fusion(s32[256]{0:T(256)S(1)} %bitcast.87, s32[256]{0:T(256)S(1)} %iota.8, s32[]{:T(128)} %constant.24.clone.1), kind=kCustom, calls=%fused_computation.74 | custom fusion | bytes 1028 | tf_op jit(solution)/shard_map/scatter | solution.py:69
  3.6 0.2 maximum_select_fusion.4
  3.9 2.7 %collective-permute-start.1 = (bf16[1,64,4,384]{3,2,1,0:T(4,128)(2,1)S(1)}, bf16[1,64,4,384]{3,2,1,0:T(4,128)(2,1)S(1)}, u32[]{:S(2)}, u32[]{:S(2)}) collective-permute-start(bf16[1,64,4,384]{3,2,1,0:T(4,128)(2,1)S(1)} %maximum_select_fusion.4), channel_id=1, source_target_pairs={{0,4},{1,5},{4,0},{5,1},{8,12},{9,13},{12,8},{13,9},{2,6},{3,7},{6... | collective-permute-start | bytes 589832 | tf_op jit(solution)/shard_map/ppermute | solution.py:18
  6.5 0.9 %fusion.51 = bf16[32,4,384]{2,1,0:T(4,128)(2,1)S(1)} fusion(bf16[1,64,4,384]{3,2,1,0:T(4,128)(2,1)} %param.5, s32[]{:T(128)S(6)} %select_n.102), kind=kLoop, calls=%fused_computation.78 | loop fusion | bytes 196612 | tf_op jit(solution)/shard_map/concatenate | solution.py:19
  7.5 0.2 maximum_select_fusion.3
  7.7 4.4 %collective-permute-done.1 = bf16[1,64,4,384]{3,2,1,0:T(4,128)(2,1)S(1)} collective-permute-done((bf16[1,64,4,384]{3,2,1,0:T(4,128)(2,1)S(1)}, bf16[1,64,4,384]{3,2,1,0:T(4,128)(2,1)S(1)}, u32[]{:S(2)}, u32[]{:S(2)}) %collective-permute-start.1) | collective-permute-done | bytes 196640 | tf_op jit(solution)/shard_map/ppermute | solution.py:18
  12.1 0.4 maximum_select_fusion.2
  12.5 2.8 %collective-permute-start.2 = (bf16[1,128,4,384]{3,2,1,0:T(4,128)(2,1)S(1)}, bf16[1,128,4,384]{3,2,1,0:T(4,128)(2,1)S(1)}, u32[]{:S(2)}, u32[]{:S(2)}) collective-permute-start(bf16[1,128,4,384]{3,2,1,0:T(4,128)(2,1)S(1)} %maximum_select_fusion.2), channel_id=1, source_target_pairs={{0,8},{1,9},{4,12},{5,13},{8,0},{9,1},{12,4},{13,5},{2,10},{3,11},... | collective-permute-start | bytes 1179656 | tf_op jit(solution)/shard_map/ppermute | solution.py:18
  15.3 0.1 broadcast_in_dim.37
  15.4 0.1 broadcast_in_dim.38
  15.6 0.1 broadcast_in_dim.39
  15.7 0.4 maximum_select_fusion.1
  16.2 16.7 %collective-permute-done.2 = bf16[1,128,4,384]{3,2,1,0:T(4,128)(2,1)S(1)} collective-permute-done((bf16[1,128,4,384]{3,2,1,0:T(4,128)(2,1)S(1)}, bf16[1,128,4,384]{3,2,1,0:T(4,128)(2,1)S(1)}, u32[]{:S(2)}, u32[]{:S(2)}) %collective-permute-start.2) | collective-permute-done | bytes 393248 | tf_op jit(solution)/shard_map/ppermute | solution.py:18
  32.8 0.9 %maximum_select_fusion = bf16[256,4,384]{2,1,0:T(4,128)(2,1)S(1)} fusion(bf16[128,4,384]{2,1,0:T(4,128)(2,1)S(1)} %bitcast.84, bf16[128,4,384]{2,1,0:T(4,128)(2,1)S(1)} %maximum_select_fusion.1, pred[]{:T(512)S(6)} %eq.9), kind=kLoop, calls=%fused_computation.37 | loop fusion | flops 1179648 | bytes 1572865 | tf_op jit(solution)/shard_map/jit(_where)/select_n | solution.py:21
  33.7 1.5 %gather_fusion = bf16[256,4,384]{2,1,0:T(4,128)(2,1)S(1)} fusion(bf16[256,4,384]{2,1,0:T(4,128)(2,1)S(1)} %maximum_select_fusion, s32[1024]{0:T(1024)S(1)} %pad_clamp_fusion), kind=kCustom, calls=%fused_computation | custom fusion | bytes 1573888 | tf_op jit(solution)/shard_map/jit(_take)/gather | solution.py:71
  35.2 0.2 gather.7
  35.4 0.5 multiply_reduce_fusion
  35.9 0.1 sqrt.29
  36.0 0.2 bitcast_convert_fusion
  36.1 0.2 fusion.22
  36.3 0.2 fusion.23
  36.5 0.2 fusion
  36.7 0.0 copy-start.2
  36.7 2.1 %convolution_convert_fusion = bf16[2,512,768]{2,1,0:T(8,128)(2,1)} fusion(bf16[2,512,384]{2,1,0:T(8,128)(2,1)S(1)} %fusion, bf16[384,768]{1,0:T(8,128)(2,1)S(1)} %copy-done), kind=kOutput, calls=%fused_computation.3 | convolution fusion | flops 604766208 | bytes 2949120 | tf_op jit(solution)/shard_map/fnc,cd->fnd/dot_general | solution.py:81
  38.9 1.9 %fusion.46 = (f32[2,256]{1,0:T(2,128)S(1)}, f32[2,256,512]{2,1,0:T(8,128)S(1)}) fusion(bf16[2,512,768]{2,1,0:T(8,128)(2,1)} %convolution_convert_fusion, bf16[2,256,384]{2,1,0:T(8,128)(2,1)S(1)} %bitcast.85, bf16[384,384]{1,0:T(8,128)(2,1)S(1)} %copy-done.2), kind=kOutput, calls=%fused_computation.77 | convolution fusion | flops 353041920 | bytes 2525184 | tf_op jit(solution)/shard_map/fqc,fkc->fqk/dot_general | solution.py:34
  40.8 0.3 fusion.19
  41.1 1.6 %convolution_divide_fusion = f32[2,256,384]{2,1,0:T(8,128)S(1)} fusion(bf16[2,512,768]{2,1,0:T(8,128)(2,1)} %convolution_convert_fusion, f32[2,256,512]{2,1,0:T(8,128)S(1)} %get-tuple-element.14, f32[2,256]{1,0:T(2,128)S(1)} %get-tuple-element.13, f32[2,256]{1,0:T(2,128)S(1)} %fusion.19), kind=kOutput, calls=%fused_computation.17 | convolution fusion | flops 202047488 | bytes 2625536 | tf_op jit(solution)/shard_map/fqk,fkc->fqc/dot_general | solution.py:40
  42.8 0.2 fusion.21
  43.0 0.3 fusion.37
  43.4 0.0 copy-start.3
  43.4 0.4 copy.34
  43.8 0.3 pad.5.clone
  44.1 0.1 slice.59
  44.2 0.5 fusion.28
  44.7 0.2 copy-done.1
  44.9 0.7 %fusion.16 = f32[2,16,9,192]{3,1,2,0:T(8,128)S(1)} fusion(bf16[3,3,3,384,192]{3,4,2,1,0:T(8,128)(2,1)S(1)} %copy-done.1, bf16[4,2,8,11,384]{4,1,3,2,0:T(2,128)(2,1)S(1)} %fusion.28, pred[16,9]{0,1:T(8,128)(4,1)S(1)} %copy-done.3), kind=kOutput, calls=%fused_computation.24 | convolution fusion | flops 382261248 | bytes 2091008 | tf_op jit(solution)/shard_map/conv_general_dilated | solution.py:45
  45.6 0.7 %fusion.13 = f32[2,16,9,192]{3,1,2,0:T(8,128)S(1)} fusion(bf16[3,3,3,384,192]{3,4,2,1,0:T(8,128)(2,1)S(1)} %copy-done.1, bf16[4,2,8,11,384]{4,1,3,2,0:T(2,128)(2,1)S(1)} %fusion.28, pred[16,9]{0,1:T(8,128)(4,1)S(1)} %copy-done.3), kind=kOutput, calls=%fused_computation.23 | convolution fusion | flops 382261248 | bytes 2091008 | tf_op jit(solution)/shard_map/conv_general_dilated | solution.py:45
  46.4 0.7 %fusion.10 = f32[2,16,9,192]{3,1,2,0:T(8,128)S(1)} fusion(bf16[3,3,3,384,192]{3,4,2,1,0:T(8,128)(2,1)S(1)} %copy-done.1, bf16[4,2,8,11,384]{4,1,3,2,0:T(2,128)(2,1)S(1)} %fusion.28, pred[16,9]{0,1:T(8,128)(4,1)S(1)} %copy-done.3), kind=kOutput, calls=%fused_computation.22 | convolution fusion | flops 382261248 | bytes 2091008 | tf_op jit(solution)/shard_map/conv_general_dilated | solution.py:45
  47.1 0.2 copy.29
  47.4 0.2 copy.25
  47.7 0.2 copy.27
  48.0 0.1 fusion.45
  48.1 3.4 %collective-permute-start.3 = (f32[2,2,64,192]{3,2,1,0:T(8,128)S(1)}, f32[2,2,64,192]{3,2,1,0:T(8,128)S(1)}, u32[]{:S(2)}, u32[]{:S(2)}) collective-permute-start(f32[2,2,64,192]{3,2,1,0:T(8,128)S(1)} %pad_maximum_fusion), channel_id=1, source_target_pairs={{0,2},{1,3},{4,6},{5,7},{8,10},{9,11},{12,14},{13,15},{16,18},{17,... | collective-permute-start | bytes 589832 | tf_op jit(solution)/shard_map/ppermute | solution.py:95
  51.5 4.6 %collective-permute-done.3 = f32[2,2,64,192]{3,2,1,0:T(8,128)S(1)} collective-permute-done((f32[2,2,64,192]{3,2,1,0:T(8,128)S(1)}, f32[2,2,64,192]{3,2,1,0:T(8,128)S(1)}, u32[]{:S(2)}, u32[]{:S(2)}) %collective-permute-start.3) | collective-permute-done | bytes 196640 | tf_op jit(solution)/shard_map/ppermute | solution.py:95
  56.1 0.8 %fusion.41 = bf16[2,2,64,192]{3,2,1,0:T(8,128)(2,1)} fusion(f32[2,2,64,192]{3,2,1,0:T(8,128)S(1)} %collective-permute-done.3, f32[1,2,64,192]{3,2,1,0:T(8,128)S(1)} %get-tuple-element.10, f32[1,2,64,192]{3,2,1,0:T(8,128)S(1)} %get-tuple-element.9, bf16[2,2,64,384]{3,2,1,0:T(8,128)(2,1)S(1)} %slice.58, s32[]{:T(128)S(6)} %select_n.112), kind=kLoop, calls=%fused_computation.56 | loop fusion | flops 245760 | bytes 589828 | tf_op jit(solution)/shard_map/convert_element_type | solution.py:100
  (23 shorter events, 0.3 us)
Async XLA Ops:
  0.0 36.7 %copy-start = (bf16[384,768]{1,0:T(8,128)(2,1)S(1)}, bf16[384,768]{1,0:T(8,128)(2,1)}, u32[]{:S(2)}) copy-start(bf16[384,768]{1,0:T(8,128)(2,1)} %param.8) | copy-start | bytes 1769476
  1.0 2.6 %collective-permute-start = (bf16[1,32,4,384]{3,2,1,0:T(4,128)(2,1)S(1)}, bf16[1,32,4,384]{3,2,1,0:T(4,128)(2,1)S(1)}, u32[]{:S(2)}, u32[]{:S(2)}) collective-permute-start(bf16[1,32,4,384]{3,2,1,0:T(4,128)(2,1)S(1)} %constant_dynamic-slice_fusion), channel_id=1, source_target_pairs={{0,1},{1,0},{4,5},{5,4},{8,9},{9,8},{12,13},{13,12},{2,3},{3,2},{6... | collective-permute-start | bytes 294920 | tf_op jit(solution)/shard_map/ppermute | solution.py:18
  3.9 8.2 %collective-permute-start.1 = (bf16[1,64,4,384]{3,2,1,0:T(4,128)(2,1)S(1)}, bf16[1,64,4,384]{3,2,1,0:T(4,128)(2,1)S(1)}, u32[]{:S(2)}, u32[]{:S(2)}) collective-permute-start(bf16[1,64,4,384]{3,2,1,0:T(4,128)(2,1)S(1)} %maximum_select_fusion.4), channel_id=1, source_target_pairs={{0,4},{1,5},{4,0},{5,1},{8,12},{9,13},{12,8},{13,9},{2,6},{3,7},{6... | collective-permute-start | bytes 589832 | tf_op jit(solution)/shard_map/ppermute | solution.py:18
  12.5 20.3 %collective-permute-start.2 = (bf16[1,128,4,384]{3,2,1,0:T(4,128)(2,1)S(1)}, bf16[1,128,4,384]{3,2,1,0:T(4,128)(2,1)S(1)}, u32[]{:S(2)}, u32[]{:S(2)}) collective-permute-start(bf16[1,128,4,384]{3,2,1,0:T(4,128)(2,1)S(1)} %maximum_select_fusion.2), channel_id=1, source_target_pairs={{0,8},{1,9},{4,12},{5,13},{8,0},{9,1},{12,4},{13,5},{2,10},{3,11},... | collective-permute-start | bytes 1179656 | tf_op jit(solution)/shard_map/ppermute | solution.py:18
  36.7 2.1 %copy-start.2 = (bf16[384,384]{1,0:T(8,128)(2,1)S(1)}, bf16[384,384]{1,0:T(8,128)(2,1)}, u32[]{:S(2)}) copy-start(bf16[384,384]{1,0:T(8,128)(2,1)} %param.7) | copy-start | bytes 884740
  42.8 2.1 %copy-start.1 = (bf16[3,3,3,384,192]{3,4,2,1,0:T(8,128)(2,1)S(1)}, bf16[3,3,3,384,192]{3,4,2,1,0:T(8,128)(2,1)}, u32[]{:S(2)}) copy-start(bf16[3,3,3,384,192]{3,4,2,1,0:T(8,128)(2,1)} %param.9) | copy-start | bytes 11943940
  43.4 1.5 %copy-start.3 = (pred[16,9]{0,1:T(8,128)(4,1)S(1)}, pred[16,9]{0,1:T(8,128)(4,1)}, u32[]{:S(2)}) copy-start(pred[16,9]{0,1:T(8,128)(4,1)} %constant.85) | copy-start | bytes 436
  48.1 8.1 %collective-permute-start.3 = (f32[2,2,64,192]{3,2,1,0:T(8,128)S(1)}, f32[2,2,64,192]{3,2,1,0:T(8,128)S(1)}, u32[]{:S(2)}, u32[]{:S(2)}) collective-permute-start(f32[2,2,64,192]{3,2,1,0:T(8,128)S(1)} %pad_maximum_fusion), channel_id=1, source_target_pairs={{0,2},{1,3},{4,6},{5,7},{8,10},{9,11},{12,14},{13,15},{16,18},{17,... | collective-permute-start | bytes 589832 | tf_op jit(solution)/shard_map/ppermute | solution.py:95
